TPU v7x, 256 devices: a whole 4x4x8 slice. The times are simulated.
256 devices in a mesh: ctx: 32 (over x, z), head: 8 (over y, core).
Axes of the slice: x: 4, y: 4, z: 8, core: 2. Of those that a mesh axis runs over, the one named last changes fastest.
Arguments:
- features: bfloat16 [8192, 16384], P('ctx', 'head'), may hold values from -6 to 6
- log_decay: float32 [256, 8192], P('head', 'ctx'), may hold values from -2 to 0, as said below
- step_size: float32 [256, 8192], P('head', 'ctx'), may hold values from 0.0002 to 0.002
- b_matrix: bfloat16 [8192, 2048], P('ctx', 'head'), may hold values from -6 to 6
- c_matrix: bfloat16 [8192, 2048], P('ctx', 'head'), may hold values from -6 to 6
- skip_gain: float32 [256], P('head'), may hold values from 0.5 to 1.5
Outputs:
- mixed: bfloat16 [8192, 16384], P('ctx', 'head')
Inputs may be any that keep to these rules, and one draw needn't show every extreme that they name: `log_decay`: every entry is negative.
All inputs are finite; a program needn't handle non-finite values.
Results may differ from a plain program's by a relative error of at most 0.0013.
Values sent between devices are 32-bit elements; how exact they have to be, the bound alone decides.
No kernel may reach another device: no remote copies, remote signals or barrier semaphores. Data moves between devices by JAX's collectives and lax.ppermute only.
A program may use at most 320 MiB of HBM per device.

v0:
```python
import jax
import jax.numpy as jnp
import numpy as np
from jax import lax
from jax.sharding import PartitionSpec as P

N = 256
SPAN = 128


def chain_mixing(decay, devices, halves):
    j = np.arange(devices)
    pos = np.stack([j, halves * devices - 1 - j], axis=1).reshape(-1)
    between = (pos[None, :, None] < pos[None, None, :]) & (pos[None, None, :] < pos[:, None, None])
    gap = jnp.sum(jnp.where(between[None], decay[:, None, None, :], 0.0), axis=-1)
    lower = pos[None, :] < pos[:, None]
    mixing = jnp.where(lower[None], jnp.exp(gap), 0.0)
    return mixing.reshape(-1, devices, halves, devices, halves)


def on_device(features, log_decay, step_size, b_matrix, c_matrix, skip_gain):
    head_count = log_decay.shape[0]
    tok_rows = features.shape[0]
    head_width = features.shape[1] // head_count
    state_size = N
    group_count = b_matrix.shape[1] // state_size
    per_group = head_count // group_count
    halves = tok_rows // SPAN
    assert halves == 2
    devices = lax.axis_size("ctx")
    per_chunk = head_count // devices
    flat = head_width * state_size
    rows = halves * head_width
    extra = 8
    cumulative = jnp.cumsum(log_decay.reshape(head_count, halves, SPAN), axis=2)
    totals = cumulative[:, :, -1]
    step_rows = step_size.reshape(head_count, halves, SPAN)
    grouped_inputs = features.reshape(halves, SPAN, group_count, per_group, head_width)
    b_spans = b_matrix.reshape(halves, SPAN, group_count, state_size)
    c_spans = c_matrix.reshape(halves, SPAN, group_count, state_size)
    coeffs = jnp.exp(totals[:, :, None] - cumulative) * step_rows
    coeffs = jnp.transpose(coeffs.reshape(group_count, per_group, halves, SPAN), (2, 3, 0, 1))
    weighted = (grouped_inputs * coeffs[..., None]).astype(jnp.bfloat16)
    span_states = jnp.einsum(
        "ksgn,ksgqp->gqkpn", b_spans, weighted, preferred_element_type=jnp.float32
    ).reshape(head_count, rows, state_size)
    me = lax.axis_index("ctx")
    spread = jnp.zeros((devices, halves, head_count), jnp.float32)
    spread = lax.dynamic_update_slice_in_dim(spread, jnp.transpose(totals)[None], me, axis=0)
    all_decay = lax.psum(spread, "ctx")
    got = lax.all_to_all(span_states, "ctx", 0, 0, tiled=True)
    got_states = got.reshape(devices, per_chunk, halves, head_width, state_size)
    mine = lax.dynamic_slice_in_dim(all_decay, me * per_chunk, per_chunk, axis=2)
    mixing = chain_mixing(
        jnp.transpose(mine, (2, 0, 1)).reshape(per_chunk, devices * halves), devices, halves
    )
    j = np.arange(devices)
    own = np.zeros((devices, halves, devices, halves), bool)
    own[j, 1, j, 0] = True
    others = jnp.where(own[None], 0.0, mixing)
    if per_chunk == 1:
        solved = jnp.einsum(
            "uv,vpn->upn",
            others.reshape(devices * halves, devices * halves),
            got.reshape(devices * halves, head_width, state_size),
            precision=lax.Precision.HIGHEST,
            preferred_element_type=jnp.float32,
        ).reshape(devices, rows, state_size)
    else:
        solved = jnp.einsum(
            "cjkJL,JcLpn->jckpn",
            others,
            got_states,
            precision=lax.Precision.HIGHEST,
            preferred_element_type=jnp.float32,
        ).reshape(devices * per_chunk, rows, state_size)
    back = lax.all_to_all(solved, "ctx", 0, 0, tiled=True)
    later = np.arange(devices)[:, None] > me
    gain = jnp.exp(jnp.sum(jnp.where(later, jnp.sum(all_decay, axis=1), 0.0), axis=0))
    state_halves = [
        back[:, :head_width].astype(jnp.bfloat16).reshape(head_count * head_width, state_size),
        (back[:, head_width:rows] + gain[:, None, None] * span_states[:, :head_width])
        .astype(jnp.bfloat16)
        .reshape(head_count * head_width, state_size),
    ]
    scores = jnp.einsum("ktgn,ksgn->gkts", c_spans, b_spans, preferred_element_type=jnp.float32)
    causal = jnp.arange(SPAN)[:, None] >= jnp.arange(SPAN)[None, :]
    cum_grouped = cumulative.reshape(group_count, per_group, halves, SPAN)
    step_grouped = step_rows.reshape(group_count, per_group, halves, SPAN)
    decay_gaps = jnp.where(causal, cum_grouped[..., :, None] - cum_grouped[..., None, :], -jnp.inf)
    weights = (scores[:, None] * jnp.exp(decay_gaps) * step_grouped[:, :, :, None, :]).astype(
        jnp.bfloat16
    )
    diagonal_part = jnp.einsum(
        "gqkts,ksgqp->ktgqp", weights, grouped_inputs, preferred_element_type=jnp.float32
    ).reshape(halves, SPAN, head_count * head_width)
    decay_in = jnp.repeat(jnp.transpose(jnp.exp(cumulative), (1, 2, 0)), head_width, axis=2)
    skip = jnp.repeat(skip_gain, head_width)[None, :]
    inputs = features.reshape(halves, SPAN, head_count * head_width).astype(jnp.float32)
    per_group_width = per_group * head_width
    outs = []
    for k in range(halves):
        state_part = jnp.concatenate(
            [
                jnp.dot(
                    c_spans[k, :, g],
                    state_halves[k][g * per_group_width : (g + 1) * per_group_width].T,
                    preferred_element_type=jnp.float32,
                )
                for g in range(group_count)
            ],
            axis=1,
        )
        outs.append(diagonal_part[k] + state_part * decay_in[k] + skip * inputs[k])
    return jnp.concatenate(outs, axis=0).astype(jnp.bfloat16)


def solution(mesh):
    placed = (
        P("ctx", "head"),
        P("head", "ctx"),
        P("head", "ctx"),
        P("ctx", "head"),
        P("ctx", "head"),
        P("head"),
    )
    return jax.shard_map(
        on_device, mesh=mesh, in_specs=placed, out_specs=P("ctx", "head"), check_vma=False
    )
```

profile of v0, /device:TPU:16, one launch (start us, length us, event | category | flops | bytes accessed | tf_op | source)
XLA Modules:
  0.0 344.3 jit_solution(12947823522675433255)
XLA Ops:
  0.0 0.8 copy_bitcast_fusion.1
  0.8 0.6 reduce_window_sum.13
  1.4 0.2 slice_reduce_fusion
  1.5 0.8 reshape.145
  2.4 1.5 copy.52
  3.9 0.3 reshape.142
  4.2 1.1 multiply_convert_fusion.2
  5.3 0.7 convolution_bitcast_fusion.2
  6.0 2.2 copy.58
  8.3 11.6 %all-to-all-start = ((f32[32,128,256]{2,1,0:T(8,128)}), f32[32,128,256]{2,1,0:T(8,128)}, u32[]{:S(2)}, u32[]{:S(2)}) async-start(f32[32,128,256]{2,1,0:T(8,128)} %bitcast.92), calls=%async_computation | async-start | bytes 8388608 | tf_op jit(solution)/shard_map/all_to_all | solution.py:51
  20.1 232.9 %psum.7 = f32[32,2,32]{1,0,2:T(8,128)S(1)} all-reduce(f32[32,2,32]{1,0,2:T(8,128)S(1)} %dynamic_update_slice.3), channel_id=1, replica_groups=mesh['ctx'=32,'head'=8] {'ctx'}, use_global_device_ids=true, to_apply=%region_1.2 | all-reduce | flops 2048 | bytes 16384 | tf_op jit(solution)/shard_map/psum | solution.py:50
  253.0 0.1 broadcast_in_dim.72
  253.1 0.6 select_reduce_fusion
  253.8 8.4 %fusion = f32[64,64,256]{2,0,1:T(8,128)S(1)} fusion(f32[64,64,256]{2,1,0:T(8,128)} %bitcast.17, pred[64,64]{1,0:T(32,128)(4,1)S(1)} %copy-done.11, pred[64,64]{1,0:T(32,128)(4,1)S(1)} %copy-done.10, f32[64,64]{1,0:T(8,128)S(1)} %select_reduce_fusion), kind=kOutput, calls=%fused_computation | convolution fusion | flops 805314560 | bytes 8413184 | tf_op jit(solution)/shard_map/uv,vpn->upn/dot_general | solution.py:62
  262.2 4.4 %copy.60 = f32[64,64,256]{2,1,0:T(8,128)} copy(f32[64,64,256]{2,0,1:T(8,128)S(1)} %fusion) | data formatting | bytes 8388608 | tf_op jit(solution)/shard_map/uv,vpn->upn/dot_general | solution.py:62
  266.6 5.2 %all-to-all-start.1 = ((f32[32,128,256]{2,1,0:T(8,128)}), f32[32,128,256]{2,1,0:T(8,128)}, u32[]{:S(2)}, u32[]{:S(2)}) async-start(f32[32,128,256]{2,1,0:T(8,128)} %bitcast.94), calls=%async_computation.1 | async-start | bytes 8388608 | tf_op jit(solution)/shard_map/all_to_all | solution.py:77
  271.8 0.2 reduce_sum.28
  272.0 0.2 convert_element_type.30
  272.3 0.1 select_reduce_fusion.1
  272.4 0.2 fusion.35
  272.6 3.6 %fusion.19 = f32[2,128,1,32,64]{1,4,3,0,2:T(8,128)S(1)} fusion(f32[32,2,128]{2,0,1:T(8,128)S(1)} %copy_bitcast_fusion, f32[32,2,128]{2,0,1:T(8,128)S(1)} %reduce_window_sum.13, f32[2,128,128]{2,1,0:T(8,128)S(1)} %fusion.35, pred[128,128]{1,0:T(8,128)(4,1)S(1)} %iota_compare_fusion, bf16[2,128,32,64]{1,0,3,2:T(2,128)(2,1)} %copy-done.2), kind=kOutput, calls=%fused_computation.27 | convolution fusion | flops 139460608 | bytes 3358720 | tf_op jit(solution)/shard_map/gqkts,ksgqp->ktgqp/dot_general | solution.py:94
  276.2 1.2 fusion.34
  277.4 1.3 copy.64
  278.8 1.3 copy.63
  280.3 2.6 copy.62
  283.0 1.3 copy.61
  284.3 53.5 %all-to-all-done.1 = f32[32,128,256]{2,1,0:T(8,128)} async-done(((f32[32,128,256]{2,1,0:T(8,128)}), f32[32,128,256]{2,1,0:T(8,128)}, u32[]{:S(2)}, u32[]{:S(2)}) %all-to-all-start.1) | async-done | bytes 4194336 | tf_op jit(solution)/shard_map/all_to_all | solution.py:77
  337.8 2.6 fusion.12
  340.4 0.5 fusion.8
  340.9 1.8 slice.95
  342.7 0.5 fusion.9
  343.3 1.1 pad_maximum_fusion
  (45 shorter events, 0.8 us)
Async XLA Ops:
  0.0 5.3 %copy-start = (bf16[256,256]{1,0:T(8,128)(2,1)S(1)}, bf16[256,256]{1,0:T(8,128)(2,1)}, u32[]{:S(2)}) copy-start(bf16[256,256]{1,0:T(8,128)(2,1)} %param.13) | copy-start | bytes 393220
  4.2 4.0 %copy-start.2 = (bf16[2,128,32,64]{1,0,3,2:T(2,128)(2,1)}, bf16[2,128,32,64]{1,0,3,2:T(2,128)(2,1)S(1)}, u32[]{:S(2)}) copy-start(bf16[2,128,32,64]{1,0,3,2:T(2,128)(2,1)S(1)} %reshape.142) | copy-start | bytes 3145732
  8.3 244.9 %copy-start.8 = (pred[1,64,64,64]{3,2,1,0:T(32,128)(4,1)S(1)}, pred[1,64,64,64]{3,2,1,0:T(32,128)(4,1)}, u32[]{:S(2)}) copy-start(pred[1,64,64,64]{3,2,1,0:T(32,128)(4,1)} %constant.26.clone) | copy-start | bytes 786436
  8.3 245.5 %copy-start.10 = (pred[64,64]{1,0:T(32,128)(4,1)S(1)}, pred[64,64]{1,0:T(32,128)(4,1)}, u32[]{:S(2)}) copy-start(pred[64,64]{1,0:T(32,128)(4,1)} %constant.31) | copy-start | bytes 12292
  8.3 245.5 %copy-start.11 = (pred[64,64]{1,0:T(32,128)(4,1)S(1)}, pred[64,64]{1,0:T(32,128)(4,1)}, u32[]{:S(2)}) copy-start(pred[64,64]{1,0:T(32,128)(4,1)} %constant.32) | copy-start | bytes 12292
  8.3 245.5 %all-to-all-start = ((f32[32,128,256]{2,1,0:T(8,128)}), f32[32,128,256]{2,1,0:T(8,128)}, u32[]{:S(2)}, u32[]{:S(2)}) async-start(f32[32,128,256]{2,1,0:T(8,128)} %bitcast.92), calls=%async_computation | async-start | bytes 8388608 | tf_op jit(solution)/shard_map/all_to_all | solution.py:51
  266.6 5.4 %copy-start.1 = (bf16[256,2048]{1,0:T(8,128)(2,1)S(1)}, bf16[256,2048]{1,0:T(8,128)(2,1)}, u32[]{:S(2)}) copy-start(bf16[256,2048]{1,0:T(8,128)(2,1)} %param.10) | copy-start | bytes 3145732
  266.6 5.7 %copy-start.13 = (s32[32,1]{0,1:T(1,128)S(1)}, s32[32,1]{0,1:T(1,128)}, u32[]{:S(2)}) copy-start(s32[32,1]{0,1:T(1,128)} %constant.29.clone) | copy-start | bytes 388
  266.6 5.8 %copy-start.9 = (f32[32,256]{1,0:T(8,128)S(1)}, f32[32,256]{1,0:T(8,128)}, u32[]{:S(2)}) copy-start(f32[32,256]{1,0:T(8,128)} %param.12) | copy-start | bytes 98308
  266.6 5.9 %copy-start.7 = (bf16[256,256]{1,0:T(8,128)(2,1)S(1)}, bf16[256,256]{1,0:T(8,128)(2,1)}, u32[]{:S(2)}) copy-start(bf16[256,256]{1,0:T(8,128)(2,1)} %param.14) | copy-start | bytes 393220
  266.6 71.2 %all-to-all-start.1 = ((f32[32,128,256]{2,1,0:T(8,128)}), f32[32,128,256]{2,1,0:T(8,128)}, u32[]{:S(2)}, u32[]{:S(2)}) async-start(f32[32,128,256]{2,1,0:T(8,128)} %bitcast.94), calls=%async_computation.1 | async-start | bytes 8388608 | tf_op jit(solution)/shard_map/all_to_all | solution.py:77
  276.2 3.9 %copy-start.12 = (f32[32]{0:T(128)S(1)}, f32[32]{0:T(128)}, u32[]{:S(2)}) copy-start(f32[32]{0:T(128)} %param.15) | copy-start | bytes 388
  284.3 56.1 %copy-start.3 = (f32[128,2048]{1,0:T(8,128)S(1)}, f32[128,2048]{1,0:T(8,128)}, u32[]{:S(2)}) copy-start(f32[128,2048]{1,0:T(8,128)} %copy.64) | copy-start | bytes 3145732
  337.8 2.6 copy-start.5
  340.4 2.4 copy-start.4
  340.4 2.4 copy-start.6
where the time goes:
time: 345 us; the launch traced here: 344 us
  blocking collectives  233 us (68%)
  waiting for transfers between devices  53.5 us (16%)
  local copies, waits for them, and re-layouts  20.4 us (6%)
  starting transfers between devices  16.8 us (5%)
  matrix products  13.9 us (4%)
  other arithmetic  6.54 us (2%)
    psum x1, blocking collectives, on_device(): all_decay = lax.psum(spread, 'ctx')  233 us
    all_to_all x1, waiting for transfers between devices, on_device(): back = lax.all_to_all(solved, 'ctx', 0, 0, tiled=True)  53.5 us
    all_to_all x1, starting transfers between devices, on_device(): got = lax.all_to_all(span_states, 'ctx', 0, 0, tiled=True)  11.6 us
    dot_general x1, matrix products, on_device(): jnp.einsum('uv,vpn->upn', others.reshape(devices * halves, devices * halv...  8.4 us
  transfers between devices with their start and end apart: 2, of which 1 were waited for; matrix products, arithmetic and copies ran while one was open for 4% of the time, Pallas kernels for 0%

commit v1 on v0

--- a/solution.py
+++ b/solution.py
@@ -47,7 +47,15 @@
     me = lax.axis_index("ctx")
     spread = jnp.zeros((devices, halves, head_count), jnp.float32)
     spread = lax.dynamic_update_slice_in_dim(spread, jnp.transpose(totals)[None], me, axis=0)
-    all_decay = lax.psum(spread, "ctx")
+
+    def take_the_tokens(block_in):
+        n_slots = lax.axis_size("ctx")
+        answer = block_in
+        for w in [[(at, at ^ c) for at in range(n_slots)] for c in (1, 2, 4, 8, 16) if c < n_slots]:
+            answer = answer + lax.ppermute(answer, "ctx", w)
+        return answer
+
+    all_decay = take_the_tokens(spread)
     got = lax.all_to_all(span_states, "ctx", 0, 0, tiled=True)
     got_states = got.reshape(devices, per_chunk, halves, head_width, state_size)
     mine = lax.dynamic_slice_in_dim(all_decay, me * per_chunk, per_chunk, axis=2)

time: 345 us -> 259 us (0.75)
  blocking collectives: 233 us -> 0 us
  waiting for transfers between devices: 53.5 us -> 181 us
  starting transfers between devices: 16.8 us -> 35.8 us
    psum x1 -> x0, blocking collectives: 233 us -> none  [on_device(): all_decay = lax.psum(spread, 'ctx')]
    ppermute x0 -> x5, waiting for transfers between devices: none -> 101 us  [take_the_tokens(): answer = answer + lax.ppermute(answer, 'ctx', w)]
    all_to_all x1, waiting for transfers between devices: 53.5 us -> 80 us  [on_device(): back = lax.all_to_all(solved, 'ctx', 0, 0, tiled=True)]
    ppermute x0 -> x5, starting transfers between devices: none -> 14.3 us  [take_the_tokens(): answer = answer + lax.ppermute(answer, 'ctx', w)]
    all_to_all x1, starting transfers between devices: 5.18 us -> 9.87 us  [on_device(): back = lax.all_to_all(solved, 'ctx', 0, 0, tiled=True)]
  transfers between devices with their start and end apart: 2 -> 7, of which waited for: 1 -> 6; matrix products, arithmetic and copies ran while one was open for 4% -> 5% of each run, Pallas kernels for 0% -> 0%
where the time goes in v1:
time: 259 us
  waiting for transfers between devices  181 us (70%)
  starting transfers between devices  35.8 us (14%)
  local copies, waits for them, and re-layouts  20.5 us (8%)
  matrix products  15.5 us (6%)
  other arithmetic  5.77 us (2%)
    ppermute x5, waiting for transfers between devices, take_the_tokens(): answer = answer + lax.ppermute(answer, 'ctx', w)  101 us
    all_to_all x1, waiting for transfers between devices, on_device(): back = lax.all_to_all(solved, 'ctx', 0, 0, tiled=True)  80 us
    ppermute x5, starting transfers between devices, take_the_tokens(): answer = answer + lax.ppermute(answer, 'ctx', w)  14.3 us
    all_to_all x1, starting transfers between devices, on_device(): got = lax.all_to_all(span_states, 'ctx', 0, 0, tiled=True)  11.6 us
    all_to_all x1, starting transfers between devices, on_device(): back = lax.all_to_all(solved, 'ctx', 0, 0, tiled=True)  9.87 us
    dot_general x1, matrix products, on_device(): jnp.einsum('uv,vpn->upn', others.reshape(devices * halves, devices * halv...  8.4 us
  transfers between devices with their start and end apart: 7, of which 6 were waited for; matrix products, arithmetic and copies ran while one was open for 5% of the time, Pallas kernels for 0%

profile of v1, /device:TPU:16, one launch (start us, length us, event | category | flops | bytes accessed | tf_op | source)
XLA Modules:
  0.0 258.7 jit_solution(16041188850117148242)
XLA Ops:
  0.0 0.8 copy_bitcast_fusion.1
  1.5 0.8 reshape.145
  2.4 1.5 copy.35
  4.2 1.1 multiply_convert_fusion.2
  5.3 0.7 convolution_bitcast_fusion.2
  6.0 2.2 copy.40
  8.3 11.6 %all-to-all-start = ((f32[32,128,256]{2,1,0:T(8,128)}), f32[32,128,256]{2,1,0:T(8,128)}, u32[]{:S(2)}, u32[]{:S(2)}) async-start(f32[32,128,256]{2,1,0:T(8,128)} %bitcast.94), calls=%async_computation | async-start | bytes 8388608 | tf_op jit(solution)/shard_map/all_to_all | solution.py:59
  19.9 1.8 collective-permute-start
  21.7 89.6 %collective-permute-done = f32[32,2,32]{2,1,0:T(2,128)S(1)} collective-permute-done((f32[32,2,32]{2,1,0:T(2,128)S(1)}, f32[32,2,32]{2,1,0:T(2,128)S(1)}, u32[]{:S(2)}, u32[]{:S(2)}) %collective-permute-start) | collective-permute-done | bytes 8224 | tf_op jit(solution)/shard_map/ppermute | solution.py:55
  111.3 3.5 %collective-permute-start.1 = (f32[32,2,32]{2,1,0:T(2,128)S(1)}, f32[32,2,32]{2,1,0:T(2,128)S(1)}, u32[]{:S(2)}, u32[]{:S(2)}) collective-permute-start(f32[32,2,32]{2,1,0:T(2,128)S(1)} %fusion.32), channel_id=1, source_target_pairs={{0,16},{8,24},{16,0},{24,8},{32,48},{40,56},{48,32},{56,40},{64,80... | collective-permute-start | bytes 24584 | tf_op jit(solution)/shard_map/ppermute | solution.py:55
  114.9 2.2 collective-permute-done.1
  117.1 4.6 %collective-permute-start.2 = (f32[32,2,32]{2,1,0:T(2,128)S(1)}, f32[32,2,32]{2,1,0:T(2,128)S(1)}, u32[]{:S(2)}, u32[]{:S(2)}) collective-permute-start(f32[32,2,32]{2,1,0:T(2,128)S(1)} %add.37), channel_id=1, source_target_pairs={{0,32},{8,40},{16,48},{24,56},{32,0},{40,8},{48,16},{56,24},{64,96... | collective-permute-start | bytes 24584 | tf_op jit(solution)/shard_map/ppermute | solution.py:55
  121.8 3.3 %collective-permute-done.2 = f32[32,2,32]{2,1,0:T(2,128)S(1)} collective-permute-done((f32[32,2,32]{2,1,0:T(2,128)S(1)}, f32[32,2,32]{2,1,0:T(2,128)S(1)}, u32[]{:S(2)}, u32[]{:S(2)}) %collective-permute-start.2) | collective-permute-done | bytes 8224 | tf_op jit(solution)/shard_map/ppermute | solution.py:55
  125.1 1.5 collective-permute-start.3
  126.6 2.8 %collective-permute-done.3 = f32[32,2,32]{2,1,0:T(2,128)S(1)} collective-permute-done((f32[32,2,32]{2,1,0:T(2,128)S(1)}, f32[32,2,32]{2,1,0:T(2,128)S(1)}, u32[]{:S(2)}, u32[]{:S(2)}) %collective-permute-start.3) | collective-permute-done | bytes 8224 | tf_op jit(solution)/shard_map/ppermute | solution.py:55
  129.4 2.8 %collective-permute-start.4 = (f32[32,2,32]{2,1,0:T(2,128)S(1)}, f32[32,2,32]{2,1,0:T(2,128)S(1)}, u32[]{:S(2)}, u32[]{:S(2)}) collective-permute-start(f32[32,2,32]{2,1,0:T(2,128)S(1)} %add.39), channel_id=1, source_target_pairs={{0,128},{8,136},{16,144},{24,152},{32,160},{40,168},{48,176},{56,1... | collective-permute-start | bytes 24584 | tf_op jit(solution)/shard_map/ppermute | solution.py:55
  132.3 2.9 %collective-permute-done.4 = f32[32,2,32]{2,1,0:T(2,128)S(1)} collective-permute-done((f32[32,2,32]{2,1,0:T(2,128)S(1)}, f32[32,2,32]{2,1,0:T(2,128)S(1)}, u32[]{:S(2)}, u32[]{:S(2)}) %collective-permute-start.4) | collective-permute-done | bytes 8224 | tf_op jit(solution)/shard_map/ppermute | solution.py:55
  135.5 0.6 select_reduce_fusion
  136.1 8.4 %fusion = f32[64,64,256]{2,0,1:T(8,128)S(1)} fusion(f32[64,64,256]{2,1,0:T(8,128)} %bitcast.18, pred[64,64]{1,0:T(32,128)(4,1)S(1)} %copy-done.10, pred[64,64]{1,0:T(32,128)(4,1)S(1)} %copy-done.9, f32[64,64]{1,0:T(8,128)S(1)} %select_reduce_fusion), kind=kOutput, calls=%fused_computation | convolution fusion | flops 805314560 | bytes 8413184 | tf_op jit(solution)/shard_map/uv,vpn->upn/dot_general | solution.py:70
  144.5 4.4 %copy.42 = f32[64,64,256]{2,1,0:T(8,128)} copy(f32[64,64,256]{2,0,1:T(8,128)S(1)} %fusion) | data formatting | bytes 8388608 | tf_op jit(solution)/shard_map/uv,vpn->upn/dot_general | solution.py:70
  148.9 9.9 %all-to-all-start.1 = ((f32[32,128,256]{2,1,0:T(8,128)}), f32[32,128,256]{2,1,0:T(8,128)}, u32[]{:S(2)}, u32[]{:S(2)}) async-start(f32[32,128,256]{2,1,0:T(8,128)} %bitcast.96), calls=%async_computation.1 | async-start | bytes 8388608 | tf_op jit(solution)/shard_map/all_to_all | solution.py:85
  159.3 3.6 %fusion.19 = f32[2,128,1,32,64]{1,4,3,0,2:T(8,128)S(1)} fusion(f32[32,2,128]{2,0,1:T(8,128)S(1)} %copy_bitcast_fusion, f32[32,2,128]{2,0,1:T(8,128)S(1)} %reduce_window_sum.13, f32[2,128,128]{2,1,0:T(8,128)S(1)} %fusion.37, pred[128,128]{1,0:T(8,128)(4,1)S(1)} %iota_compare_fusion, bf16[2,128,32,64]{1,0,3,2:T(2,128)(2,1)} %copy-done.3), kind=kOutput, calls=%fused_computation.27 | convolution fusion | flops 139460608 | bytes 3358720 | tf_op jit(solution)/shard_map/gqkts,ksgqp->ktgqp/dot_general | solution.py:102
  162.9 1.2 fusion.36
  164.1 1.3 copy.44
  165.5 1.3 copy.43
  167.0 2.6 %copy.46 = f32[128,2048]{1,0:T(8,128)} copy(f32[128,2048]{0,1:T(8,128)} %bitcast.99) | data formatting | bytes 2097152 | tf_op jit(solution)/shard_map/squeeze | solution.py:122
  169.7 1.3 copy.45
  171.1 80.0 %all-to-all-done.1 = f32[32,128,256]{2,1,0:T(8,128)} async-done(((f32[32,128,256]{2,1,0:T(8,128)}), f32[32,128,256]{2,1,0:T(8,128)}, u32[]{:S(2)}, u32[]{:S(2)}) %all-to-all-start.1) | async-done | bytes 4194336 | tf_op jit(solution)/shard_map/all_to_all | solution.py:85
  251.1 1.9 slice.95
  253.0 2.2 fusion.9
  255.2 1.9 fusion.12
  257.6 1.1 pad_maximum_fusion
  (55 shorter events, 3.0 us)
Async XLA Ops:
  0.0 5.3 %copy-start = (bf16[256,256]{1,0:T(8,128)(2,1)S(1)}, bf16[256,256]{1,0:T(8,128)(2,1)}, u32[]{:S(2)}) copy-start(bf16[256,256]{1,0:T(8,128)(2,1)} %param.13) | copy-start | bytes 393220
  4.2 4.0 %copy-start.3 = (bf16[2,128,32,64]{1,0,3,2:T(2,128)(2,1)}, bf16[2,128,32,64]{1,0,3,2:T(2,128)(2,1)S(1)}, u32[]{:S(2)}) copy-start(bf16[2,128,32,64]{1,0,3,2:T(2,128)(2,1)S(1)} %reshape.142) | copy-start | bytes 3145732
  8.3 127.2 %copy-start.7 = (pred[1,64,64,64]{3,2,1,0:T(32,128)(4,1)S(1)}, pred[1,64,64,64]{3,2,1,0:T(32,128)(4,1)}, u32[]{:S(2)}) copy-start(pred[1,64,64,64]{3,2,1,0:T(32,128)(4,1)} %constant.26.clone) | copy-start | bytes 786436
  8.3 127.9 %copy-start.9 = (pred[64,64]{1,0:T(32,128)(4,1)S(1)}, pred[64,64]{1,0:T(32,128)(4,1)}, u32[]{:S(2)}) copy-start(pred[64,64]{1,0:T(32,128)(4,1)} %constant.31) | copy-start | bytes 12292
  8.3 127.9 %copy-start.10 = (pred[64,64]{1,0:T(32,128)(4,1)S(1)}, pred[64,64]{1,0:T(32,128)(4,1)}, u32[]{:S(2)}) copy-start(pred[64,64]{1,0:T(32,128)(4,1)} %constant.32) | copy-start | bytes 12292
  8.3 127.8 %all-to-all-start = ((f32[32,128,256]{2,1,0:T(8,128)}), f32[32,128,256]{2,1,0:T(8,128)}, u32[]{:S(2)}, u32[]{:S(2)}) async-start(f32[32,128,256]{2,1,0:T(8,128)} %bitcast.94), calls=%async_computation | async-start | bytes 8388608 | tf_op jit(solution)/shard_map/all_to_all | solution.py:59
  19.9 91.4 %collective-permute-start = (f32[32,2,32]{2,1,0:T(2,128)S(1)}, f32[32,2,32]{2,1,0:T(2,128)S(1)}, u32[]{:S(2)}, u32[]{:S(2)}) collective-permute-start(f32[32,2,32]{2,1,0:T(2,128)S(1)} %bitcast_dynamic-update-slice_fusion), channel_id=1, source_target_pairs={{0,8},{8,0},{16,24},{24,16},{32,40},{40,32},{48,56},{56,48},{64,72... | collective-permute-start | bytes 24584 | tf_op jit(solution)/shard_map/ppermute | solution.py:55
  111.3 5.8 %collective-permute-start.1 = (f32[32,2,32]{2,1,0:T(2,128)S(1)}, f32[32,2,32]{2,1,0:T(2,128)S(1)}, u32[]{:S(2)}, u32[]{:S(2)}) collective-permute-start(f32[32,2,32]{2,1,0:T(2,128)S(1)} %fusion.32), channel_id=1, source_target_pairs={{0,16},{8,24},{16,0},{24,8},{32,48},{40,56},{48,32},{56,40},{64,80... | collective-permute-start | bytes 24584 | tf_op jit(solution)/shard_map/ppermute | solution.py:55
  117.1 7.9 %collective-permute-start.2 = (f32[32,2,32]{2,1,0:T(2,128)S(1)}, f32[32,2,32]{2,1,0:T(2,128)S(1)}, u32[]{:S(2)}, u32[]{:S(2)}) collective-permute-start(f32[32,2,32]{2,1,0:T(2,128)S(1)} %add.37), channel_id=1, source_target_pairs={{0,32},{8,40},{16,48},{24,56},{32,0},{40,8},{48,16},{56,24},{64,96... | collective-permute-start | bytes 24584 | tf_op jit(solution)/shard_map/ppermute | solution.py:55
  125.1 4.3 %collective-permute-start.3 = (f32[32,2,32]{2,1,0:T(2,128)S(1)}, f32[32,2,32]{2,1,0:T(2,128)S(1)}, u32[]{:S(2)}, u32[]{:S(2)}) collective-permute-start(f32[32,2,32]{2,1,0:T(2,128)S(1)} %add.38), channel_id=1, source_target_pairs={{0,64},{8,72},{16,80},{24,88},{32,96},{40,104},{48,112},{56,120},{... | collective-permute-start | bytes 24584 | tf_op jit(solution)/shard_map/ppermute | solution.py:55
  129.4 5.7 %collective-permute-start.4 = (f32[32,2,32]{2,1,0:T(2,128)S(1)}, f32[32,2,32]{2,1,0:T(2,128)S(1)}, u32[]{:S(2)}, u32[]{:S(2)}) collective-permute-start(f32[32,2,32]{2,1,0:T(2,128)S(1)} %add.39), channel_id=1, source_target_pairs={{0,128},{8,136},{16,144},{24,152},{32,160},{40,168},{48,176},{56,1... | collective-permute-start | bytes 24584 | tf_op jit(solution)/shard_map/ppermute | solution.py:55
  148.9 9.9 %copy-start.2 = (bf16[256,2048]{1,0:T(8,128)(2,1)S(1)}, bf16[256,2048]{1,0:T(8,128)(2,1)}, u32[]{:S(2)}) copy-start(bf16[256,2048]{1,0:T(8,128)(2,1)} %param.10) | copy-start | bytes 3145732
  148.9 10.2 %copy-start.8 = (f32[32,256]{1,0:T(8,128)S(1)}, f32[32,256]{1,0:T(8,128)}, u32[]{:S(2)}) copy-start(f32[32,256]{1,0:T(8,128)} %param.12) | copy-start | bytes 98308
  148.9 10.2 %copy-start.6 = (bf16[256,256]{1,0:T(8,128)(2,1)S(1)}, bf16[256,256]{1,0:T(8,128)(2,1)}, u32[]{:S(2)}) copy-start(bf16[256,256]{1,0:T(8,128)(2,1)} %param.14) | copy-start | bytes 393220
  148.9 102.2 %all-to-all-start.1 = ((f32[32,128,256]{2,1,0:T(8,128)}), f32[32,128,256]{2,1,0:T(8,128)}, u32[]{:S(2)}, u32[]{:S(2)}) async-start(f32[32,128,256]{2,1,0:T(8,128)} %bitcast.96), calls=%async_computation.1 | async-start | bytes 8388608 | tf_op jit(solution)/shard_map/all_to_all | solution.py:85
  162.9 4.0 %copy-start.11 = (f32[32]{0:T(128)S(1)}, f32[32]{0:T(128)}, u32[]{:S(2)}) copy-start(f32[32]{0:T(128)} %param.15) | copy-start | bytes 388
  165.4 5.5 %copy-start.12 = (s32[32,1]{0,1:T(1,128)S(1)}, s32[32,1]{0,1:T(1,128)}, u32[]{:S(2)}) copy-start(s32[32,1]{0,1:T(1,128)} %constant.29.clone) | copy-start | bytes 388
  251.1 4.1 %copy-start.1 = (f32[1,32,2,64,256]{4,3,2,1,0:T(8,128)S(1)}, f32[1,32,2,64,256]{4,3,2,1,0:T(8,128)}, u32[]{:S(2)}) copy-start(f32[1,32,2,64,256]{4,3,2,1,0:T(8,128)} %copy.40) | copy-start | bytes 12582916
  253.0 4.1 %copy-start.4 = (f32[128,2048]{1,0:T(8,128)S(1)}, f32[128,2048]{1,0:T(8,128)}, u32[]{:S(2)}) copy-start(f32[128,2048]{1,0:T(8,128)} %copy.46) | copy-start | bytes 3145732
  253.0 4.1 %copy-start.5 = (f32[128,2048]{1,0:T(8,128)S(1)}, f32[128,2048]{1,0:T(8,128)}, u32[]{:S(2)}) copy-start(f32[128,2048]{1,0:T(8,128)} %copy.45) | copy-start | bytes 3145732
